TPU v7x, 32 devices: a whole 2x2x4 slice. The times are simulated.
32 devices in a mesh: group: 2 (over y), ctx: 8 (over z, x), tsp: 2 (over core).
Axes of the slice: x: 2, y: 2, z: 4, core: 2. Of those that a mesh axis runs over, the one named last changes fastest.
Arguments:
- query_proj: bfloat16 [4096, 2048], P(('group', 'ctx'), 'tsp'), parts along dimension 0, may hold values from -8 to 8
- key_proj: bfloat16 [4096, 1024], P(('group', 'ctx'), 'tsp'), parts along dimension 0, may hold values from -8 to 8
- value_projection: bfloat16 [4096, 1024], P(('group', 'ctx'), 'tsp'), parts along dimension 0, may hold values from -6 to 6
- grad_out: bfloat16 [4096, 2048], P(('group', 'ctx', 'tsp')), parts along dimension 0, may hold values from -6 to 6
- doc_ids: int32 [4096], P(('group', 'ctx')), parts along dimension 0, may hold values from 0 to 3, never falling along the last dimension, each value on 1 to 1024 neighbouring positions
- advantages: float32 [8], P('group'), parts along dimension 0, may hold values from -4 to 4
- head_window: int32 [16], P('tsp'), may hold values from 512 to 1024, as said below
Outputs:
- query_grad: bfloat16 [4096, 2048], P(('group', 'ctx'), 'tsp'), parts along dimension 0
- key_grad: bfloat16 [4096, 1024], P(('group', 'ctx'), 'tsp'), parts along dimension 0
- value_grad: bfloat16 [4096, 1024], P(('group', 'ctx'), 'tsp'), parts along dimension 0
There are 2 independent parts, one for each index of `group`. A program takes and returns all parts, laid end to end along the dimension named above; an argument that names none is the same for every part. Nothing has to cross between parts.
Inputs may be any that keep to these rules, and one draw needn't show every extreme that they name: `doc_ids`: document numbers never fall along the sequence; every document holds 1 to 1024 positions. `head_window`: some head has a window of exactly 1024.
All inputs are finite; a program needn't handle non-finite values.
Results may differ from a plain program's by a relative error of at most 0.039.
Values may be sent and summed in bfloat16 or wider, within the bound.
No kernel may reach another device: no remote copies, remote signals or barrier semaphores. Data moves between devices by JAX's collectives and lax.ppermute only.
A program may use at most 64 MiB of HBM per device.

v0:
```python
import functools
import jax
import jax.numpy as jnp
from jax import lax
from jax.experimental import pallas as pl
from jax.experimental.pallas import tpu as pltpu
from jax.sharding import PartitionSpec as P

HEAD_DIMENSION = 128
WINDOW = 1024
ID_ROWS = 16
score_scale = 168.0 ** (-0.5)


def _nt(a, b):
    return lax.dot_general(a, b, (((1,), (1,)), ((), ())), preferred_element_type=jnp.float32)


def _tn(a, b):
    return lax.dot_general(a, b, (((0,), (0,)), ((), ())), preferred_element_type=jnp.float32)


def _nn(a, b):
    return lax.dot_general(a, b, (((1,), (0,)), ((), ())), preferred_element_type=jnp.float32)


def attention_kernel(win_ref, odd_ref, qid_ref, q_ref, g_ref, *rest, group_size):
    r1, r2, r3, r4, r5, own = rest[:6]
    dq_ref, p4_ref, p2_ref, p1_ref, p3_ref, b3_ref, own_ref = rest[6:]
    d = HEAD_DIMENSION
    rows = q_ref.shape[0]
    width = own.shape[1] // 2
    odd = odd_ref[0] == 1

    def pick(odd_source, even_source):
        def load(index):
            return jnp.where(odd, odd_source[index], even_source[index])

        return load

    def plain(ref):
        def load(index):
            return ref[index]

        return load

    sources = [plain(r4), pick(r3, r5), plain(r2), pick(r1, r3), plain(own)]
    pieces = len(sources)
    key_count = pieces * rows
    row = lax.broadcasted_iota(jnp.int32, (rows, key_count), 0)
    col = lax.broadcasted_iota(jnp.int32, (rows, key_count), 1)
    offset = row + (key_count - rows) - col
    key_ids = jnp.concatenate(
        [src((slice(rows, rows + 1), slice(0, rows))).astype(jnp.float32) for src in sources], axis=1
    )
    base_live = (offset >= 0) & (key_ids == qid_ref[...])
    for kv in range(width // d):
        keys = [src((slice(0, rows), slice(kv * d, (kv + 1) * d))) for src in sources]
        values = [src((slice(0, rows), slice(width + kv * d, width + (kv + 1) * d))) for src in sources]
        parts = kv_head(win_ref, q_ref, g_ref, dq_ref, keys, values, offset, base_live, kv, group_size)
        kcols = slice(kv * d, (kv + 1) * d)
        vcols = slice(width + kv * d, width + (kv + 1) * d)
        for target, p in ((p4_ref, 0), (p2_ref, 2), (p1_ref, 3), (p3_ref, 1)):
            target[:, kcols] = parts[p][0].astype(target.dtype)
            target[:, vcols] = parts[p][1].astype(target.dtype)
        b3_ref[:, kcols] = jnp.where(odd, parts[1][0], parts[3][0]).astype(b3_ref.dtype)
        b3_ref[:, vcols] = jnp.where(odd, parts[1][1], parts[3][1]).astype(b3_ref.dtype)
        own_ref[:, kcols] = parts[4][0]
        own_ref[:, vcols] = parts[4][1]


def kv_head(win_ref, q_ref, g_ref, dq_ref, keys, values, offset, base_live, kv, group_size):
    d = HEAD_DIMENSION
    pieces = len(keys)
    piece_rows = q_ref.shape[0]
    key_acc = [jnp.zeros((piece_rows, d), jnp.float32) for _ in range(pieces)]
    value_acc = [jnp.zeros((piece_rows, d), jnp.float32) for _ in range(pieces)]
    for h in range(group_size):
        head = kv * group_size + h
        query = q_ref[:, head * d : (head + 1) * d]
        grad = g_ref[:, head * d : (head + 1) * d]
        scores = jnp.concatenate([_nt(query, key) for key in keys], axis=1) * score_scale
        live = base_live & (offset < win_ref[head])
        scores = jnp.where(live, scores, jnp.float32(-1e30))
        top = jnp.max(scores, axis=1, keepdims=True)
        prob = jnp.exp(scores - top)
        prob = prob / jnp.sum(prob, axis=1, keepdims=True)
        prob_low = prob.astype(jnp.bfloat16)
        attended = _nn(prob_low[:, :piece_rows], values[0])
        for p in range(1, pieces):
            attended = attended + _nn(prob_low[:, p * piece_rows : (p + 1) * piece_rows], values[p])
        attended = attended.astype(jnp.bfloat16).astype(jnp.float32)
        delta = jnp.sum(grad.astype(jnp.float32) * attended, axis=1, keepdims=True)
        dprob = jnp.concatenate([_nt(grad, value) for value in values], axis=1)
        dscore = (prob * (dprob - delta)).astype(jnp.bfloat16)
        query_acc = _nn(dscore[:, :piece_rows], keys[0])
        for p in range(1, pieces):
            query_acc = query_acc + _nn(dscore[:, p * piece_rows : (p + 1) * piece_rows], keys[p])
        dq_ref[:, head * d : (head + 1) * d] = (query_acc * score_scale).astype(dq_ref.dtype)
        for p in range(pieces):
            cols = slice(p * piece_rows, (p + 1) * piece_rows)
            key_acc[p] = key_acc[p] + _tn(dscore[:, cols], query)
            value_acc[p] = value_acc[p] + _tn(prob_low[:, cols], grad)
    return [(key_acc[p] * score_scale, value_acc[p]) for p in range(pieces)]


def head_group_grads(windows, odd, query_ids, query, grad, payloads):
    rows = query.shape[0]
    pair_width = payloads[0].shape[1]
    group_size = 2 * query.shape[1] // pair_width
    vmem = pl.BlockSpec(memory_space=pltpu.VMEM)
    smem = pl.BlockSpec(memory_space=pltpu.SMEM)
    wide = jax.ShapeDtypeStruct((rows, pair_width), jnp.float32)
    low = jax.ShapeDtypeStruct((rows, pair_width), jnp.bfloat16)
    out_shape = [jax.ShapeDtypeStruct(query.shape, jnp.bfloat16), wide, wide, low, low, low, wide]
    kernel = functools.partial(attention_kernel, group_size=group_size)
    return pl.pallas_call(
        kernel,
        out_shape=out_shape,
        in_specs=[smem, smem] + [vmem] * (3 + len(payloads)),
        out_specs=[vmem] * len(out_shape),
        name="attention_group",
    )(windows, odd, query_ids, query, grad, *payloads)


def permuted(value, axis, pairs):
    return lax.ppermute(value, axis, [pair for pair in pairs if 0 <= pair[1] < lax.axis_size(axis)])


def device_body(query_proj, key_proj, value_projection, grad_out, doc_ids, advantages, head_window):
    tok_rows = query_proj.shape[0]
    kv_width = key_proj.shape[1]
    count = lax.axis_size("ctx")
    assert WINDOW // tok_rows == 4 and count % 2 == 0
    index = lax.axis_index("ctx")
    odd = (index % 2).astype(jnp.int32).reshape(1)
    doc_count = advantages.shape[0]
    matches = doc_ids[:, None] == jnp.arange(doc_count, dtype=jnp.int32)[None, :]
    token_weight = jnp.sum(jnp.where(matches, advantages[None, :], jnp.float32(0.0)), axis=1)
    grad_local = lax.all_to_all(grad_out, "tsp", split_axis=1, concat_axis=0, tiled=True)
    weighted = (token_weight[:, None] * grad_local.astype(jnp.float32)).astype(jnp.bfloat16)
    query_ids = (doc_ids + 1).astype(jnp.float32)[:, None]

    paired = jnp.concatenate([key_proj, value_projection], axis=1)
    id_rows = jnp.zeros((ID_ROWS, 2 * kv_width), jnp.bfloat16)
    id_rows = id_rows.at[0, :tok_rows].set((doc_ids + 1).astype(jnp.bfloat16))
    payload = jnp.concatenate([paired, id_rows], axis=0)

    evens = range(0, count, 2)
    odds = range(1, count, 2)
    everyone = range(count)
    swap = [(c, c + 1) for c in evens] + [(c, c - 1) for c in odds]
    got1 = permuted(payload, "ctx", [(c, c + 1) for c in evens])
    got2 = permuted(payload, "ctx", [(c, c + 2) for c in everyone])
    got3 = permuted(got2, "ctx", swap)
    got4 = permuted(got2, "ctx", [(c, c + 2) for c in everyone])
    got5 = permuted(got4, "ctx", [(c, c - 1) for c in odds])

    query_grad, part4, part2, part1, part3, back3, own_part = head_group_grads(
        head_window, odd, query_ids, query_proj, weighted, [got1, got2, got3, got4, got5, payload]
    )
    from5 = permuted(part3, "ctx", [(c, c + 1) for c in evens])
    from3 = permuted(back3, "ctx", swap)
    from1 = permuted(part1, "ctx", [(c, c - 1) for c in odds])
    send4 = (part4 + from5.astype(jnp.float32)).astype(jnp.bfloat16)
    from4 = permuted(send4, "ctx", [(c, c - 2) for c in everyone])
    send2 = (part2 + from4.astype(jnp.float32) + from3.astype(jnp.float32)).astype(jnp.bfloat16)
    from2 = permuted(send2, "ctx", [(c, c - 2) for c in everyone])
    summed = own_part + from2.astype(jnp.float32) + from1.astype(jnp.float32)
    key_grad = summed[:, :kv_width].astype(jnp.bfloat16)
    value_grad = summed[:, kv_width:].astype(jnp.bfloat16)
    return (query_grad, key_grad, value_grad)


def solution(mesh):
    in_specs = (
        P(("group", "ctx"), "tsp"),
        P(("group", "ctx"), "tsp"),
        P(("group", "ctx"), "tsp"),
        P(("group", "ctx", "tsp"), None),
        P(("group", "ctx")),
        P("group"),
        P("tsp"),
    )
    out_specs = (P(("group", "ctx"), "tsp"), P(("group", "ctx"), "tsp"), P(("group", "ctx"), "tsp"))
    return jax.shard_map(
        device_body, mesh=mesh, in_specs=in_specs, out_specs=out_specs, check_vma=False
    )
```

profile of v0, /device:TPU:8, one launch (start us, length us, event | category | flops | bytes accessed | tf_op | source)
XLA Modules:
  0.0 110.4 jit_solution(10453727218487817461)
XLA Ops:
  0.6 0.0 copy-start.7
  0.6 0.7 add_convert_fusion.3
  1.4 1.1 fusion.2.rest_5_
  2.5 0.0 copy-start
  2.5 3.5 %collective-permute-start.1 = (bf16[272,1024]{1,0:T(8,128)(2,1)S(1)}, bf16[272,1024]{1,0:T(8,128)(2,1)S(1)}, u32[]{:S(2)}, u32[]{:S(2)}) collective-permute-start(bf16[272,1024]{1,0:T(8,128)(2,1)S(1)} %fusion.2.rest_5_), channel_id=1, source_target_pairs={{0,4},{2,6},{4,8},{6,10},{8,12},{10,14},{1,5},{3,7},{5,9},{7,11},{... | collective-permute-start | bytes 1671176 | tf_op jit(solution)/shard_map/ppermute | solution.py:127
  6.0 12.8 %collective-permute-done.1.rest_1_ = bf16[272,1024]{1,0:T(8,128)(2,1)S(1)} collective-permute-done((bf16[272,1024]{1,0:T(8,128)(2,1)S(1)}, bf16[272,1024]{1,0:T(8,128)(2,1)S(1)}, u32[]{:S(2)}, u32[]{:S(2)}) %collective-permute-start.1) | collective-permute-done | bytes 557088 | tf_op jit(solution)/shard_map/ppermute | solution.py:127
  18.7 0.0 copy-start.3
  18.7 3.5 %collective-permute-start.3 = (bf16[272,1024]{1,0:T(8,128)(2,1)S(1)}, bf16[272,1024]{1,0:T(8,128)(2,1)S(1)}, u32[]{:S(2)}, u32[]{:S(2)}) collective-permute-start(bf16[272,1024]{1,0:T(8,128)(2,1)S(1)} %collective-permute-done.1.rest_1_), channel_id=1, source_target_pairs={{0,4},{2,6},{4,8},{6,10},{8,12},{10,14},{1,5},{3,7},{5,9},{7,11},{... | collective-permute-start | bytes 1671176 | tf_op jit(solution)/shard_map/ppermute | solution.py:127
  22.2 3.4 %collective-permute-start = (bf16[272,1024]{1,0:T(8,128)(2,1)S(1)}, bf16[272,1024]{1,0:T(8,128)(2,1)S(1)}, u32[]{:S(2)}, u32[]{:S(2)}) collective-permute-start(bf16[272,1024]{1,0:T(8,128)(2,1)S(1)} %fusion.2.rest_5_), channel_id=1, source_target_pairs={{0,2},{4,6},{8,10},{12,14},{1,3},{5,7},{9,11},{13,15},{16,18},{20,... | collective-permute-start | bytes 1671176 | tf_op jit(solution)/shard_map/ppermute | solution.py:127
  25.7 0.1 collective-permute-start.2
  25.7 8.4 %collective-permute-done.3.rest_3_ = bf16[272,1024]{1,0:T(8,128)(2,1)S(1)} collective-permute-done((bf16[272,1024]{1,0:T(8,128)(2,1)S(1)}, bf16[272,1024]{1,0:T(8,128)(2,1)S(1)}, u32[]{:S(2)}, u32[]{:S(2)}) %collective-permute-start.3) | collective-permute-done | bytes 557088 | tf_op jit(solution)/shard_map/ppermute | solution.py:127
  34.1 0.0 copy-start.4
  34.1 1.3 %collective-permute-start.4 = (bf16[272,1024]{1,0:T(8,128)(2,1)S(1)}, bf16[272,1024]{1,0:T(8,128)(2,1)}, u32[]{:S(2)}, u32[]{:S(2)}) collective-permute-start(bf16[272,1024]{1,0:T(8,128)(2,1)S(1)} %collective-permute-done.3.rest_3_), channel_id=1, source_target_pairs={{2,0},{6,4},{10,8},{14,12},{3,1},{7,5},{11,9},{15,13},{18,16},{22,... | collective-permute-start | bytes 1671176 | tf_op jit(solution)/shard_map/ppermute | solution.py:127
  35.4 0.0 copy-done.7
  35.4 0.0 copy-start.8
  35.5 0.0 copy-start.9
  35.5 0.8 copy.17
  36.3 0.0 copy-done
  36.3 0.0 copy-done.3
  36.3 0.0 copy-done.4
  36.3 3.5 %all-to-all-start = ((bf16[128,2,1024]{2,0,1:T(8,128)(2,1)}), bf16[128,2,1024]{2,0,1:T(8,128)(2,1)S(1)}, u32[]{:S(2)}, u32[]{:S(2)}) async-start(bf16[128,2,1024]{2,0,1:T(8,128)(2,1)} %bitcast.11), calls=%async_computation | async-start | bytes 1048576 | tf_op jit(solution)/shard_map/all_to_all | solution.py:140
  39.8 0.8 copy.14.qid_ref
  40.6 0.0 copy-done.8
  40.6 0.0 copy-done.9
  40.6 0.1 select_reduce_fusion
  40.7 0.8 all-to-all-done
  41.5 1.0 fusion.1.g_ref
  42.5 0.0 collective-permute-done.rest_0_
  42.5 0.0 copy-start.5
  42.5 5.8 %collective-permute-done.2.rest_2_ = bf16[272,1024]{1,0:T(8,128)(2,1)S(1)} collective-permute-done((bf16[272,1024]{1,0:T(8,128)(2,1)S(1)}, bf16[272,1024]{1,0:T(8,128)(2,1)S(1)}, u32[]{:S(2)}, u32[]{:S(2)}) %collective-permute-start.2) | collective-permute-done | bytes 557088 | tf_op jit(solution)/shard_map/ppermute | solution.py:127
  48.3 0.0 copy-start.6
  48.3 2.4 %collective-permute-done.4.rest_4_ = bf16[272,1024]{1,0:T(8,128)(2,1)} collective-permute-done((bf16[272,1024]{1,0:T(8,128)(2,1)S(1)}, bf16[272,1024]{1,0:T(8,128)(2,1)}, u32[]{:S(2)}, u32[]{:S(2)}) %collective-permute-start.4) | collective-permute-done | bytes 557088 | tf_op jit(solution)/shard_map/ppermute | solution.py:127
  50.7 0.0 copy-done.5
  50.7 0.0 copy-done.6
  50.7 16.8 %attention_group.1 = (bf16[256,1024]{1,0:T(8,128)(2,1)}, f32[256,1024]{1,0:T(8,128)}, f32[256,1024]{1,0:T(8,128)}, bf16[256,1024]{1,0:T(8,128)(2,1)}, bf16[256,1...) custom-call(s32[8]{0:T(128)} %win_ref.1, s32[1]{0:T(128)} %bitcast.odd_ref, ...), custom_call_target="tpu_custom_call" | custom-call | tf_op jit(solution)/shard_map/attention_group/pallas_call | solution.py:117
  67.6 2.8 %collective-permute-start.5 = (bf16[256,1024]{1,0:T(8,128)(2,1)}, bf16[256,1024]{1,0:T(8,128)(2,1)S(1)}, u32[]{:S(2)}, u32[]{:S(2)}) collective-permute-start(bf16[256,1024]{1,0:T(8,128)(2,1)} %get-tuple-element.26), channel_id=1, source_target_pairs={{0,2},{4,6},{8,10},{12,14},{1,3},{5,7},{9,11},{13,15},{16,18},{20,... | collective-permute-start | bytes 1572872 | tf_op jit(solution)/shard_map/ppermute | solution.py:127
  70.4 0.1 collective-permute-start.7
  70.4 12.5 %collective-permute-done.5 = bf16[256,1024]{1,0:T(8,128)(2,1)S(1)} collective-permute-done((bf16[256,1024]{1,0:T(8,128)(2,1)}, bf16[256,1024]{1,0:T(8,128)(2,1)S(1)}, u32[]{:S(2)}, u32[]{:S(2)}) %collective-permute-start.5) | collective-permute-done | bytes 524320 | tf_op jit(solution)/shard_map/ppermute | solution.py:127
  82.9 0.0 copy-start.10
  83.0 0.0 copy-start.2
  83.0 1.5 %add_convert_fusion.2 = bf16[256,1024]{1,0:T(8,128)(2,1)S(1)} fusion(f32[256,1024]{1,0:T(8,128)} %get-tuple-element.25, bf16[256,1024]{1,0:T(8,128)(2,1)S(1)} %collective-permute-done.5), kind=kLoop, calls=%fused_computation.6 | loop fusion | flops 786432 | bytes 2097152 | tf_op jit(solution)/shard_map/convert_element_type | solution.py:165
  84.4 2.4 %collective-permute-start.6 = (bf16[256,1024]{1,0:T(8,128)(2,1)S(1)}, bf16[256,1024]{1,0:T(8,128)(2,1)S(1)}, u32[]{:S(2)}, u32[]{:S(2)}) collective-permute-start(bf16[256,1024]{1,0:T(8,128)(2,1)S(1)} %add_convert_fusion.2), channel_id=1, source_target_pairs={{4,0},{6,2},{8,4},{10,6},{12,8},{14,10},{5,1},{7,3},{9,5},{11,7},{... | collective-permute-start | bytes 1572872 | tf_op jit(solution)/shard_map/ppermute | solution.py:127
  86.9 0.0 copy-done.10
  86.9 1.3 %collective-permute-start.9 = (bf16[256,1024]{1,0:T(8,128)(2,1)S(1)}, bf16[256,1024]{1,0:T(8,128)(2,1)S(1)}, u32[]{:S(2)}, u32[]{:S(2)}) collective-permute-start(bf16[256,1024]{1,0:T(8,128)(2,1)S(1)} %copy-done.10), channel_id=1, source_target_pairs={{2,0},{6,4},{10,8},{14,12},{3,1},{7,5},{11,9},{15,13},{18,16},{22,... | collective-permute-start | bytes 1572872 | tf_op jit(solution)/shard_map/ppermute | solution.py:127
  88.2 2.9 %collective-permute-done.7 = bf16[256,1024]{1,0:T(8,128)(2,1)S(1)} collective-permute-done((bf16[256,1024]{1,0:T(8,128)(2,1)}, bf16[256,1024]{1,0:T(8,128)(2,1)S(1)}, u32[]{:S(2)}, u32[]{:S(2)}) %collective-permute-start.7) | collective-permute-done | bytes 524320 | tf_op jit(solution)/shard_map/ppermute | solution.py:127
  91.1 6.8 %collective-permute-done.6 = bf16[256,1024]{1,0:T(8,128)(2,1)S(1)} collective-permute-done((bf16[256,1024]{1,0:T(8,128)(2,1)S(1)}, bf16[256,1024]{1,0:T(8,128)(2,1)S(1)}, u32[]{:S(2)}, u32[]{:S(2)}) %collective-permute-start.6) | collective-permute-done | bytes 524320 | tf_op jit(solution)/shard_map/ppermute | solution.py:127
  97.9 0.0 copy-done.2
  97.9 0.0 copy-start.1
  97.9 0.2 add_convert_fusion.1
  98.2 2.6 %collective-permute-start.8 = (bf16[256,1024]{1,0:T(8,128)(2,1)S(1)}, bf16[256,1024]{1,0:T(8,128)(2,1)S(1)}, u32[]{:S(2)}, u32[]{:S(2)}) collective-permute-start(bf16[256,1024]{1,0:T(8,128)(2,1)S(1)} %add_convert_fusion.1), channel_id=1, source_target_pairs={{4,0},{6,2},{8,4},{10,6},{12,8},{14,10},{5,1},{7,3},{9,5},{11,7},{... | collective-permute-start | bytes 1572872 | tf_op jit(solution)/shard_map/ppermute | solution.py:127
  100.8 0.0 collective-permute-done.9
  100.8 8.6 %collective-permute-done.8 = bf16[256,1024]{1,0:T(8,128)(2,1)S(1)} collective-permute-done((bf16[256,1024]{1,0:T(8,128)(2,1)S(1)}, bf16[256,1024]{1,0:T(8,128)(2,1)S(1)}, u32[]{:S(2)}, u32[]{:S(2)}) %collective-permute-start.8) | collective-permute-done | bytes 524320 | tf_op jit(solution)/shard_map/ppermute | solution.py:127
  109.4 0.0 copy-done.1
  109.4 0.2 add_convert_fusion
  109.6 0.8 fusion.3
  (1 shorter events, 0.0 us)
Async XLA Ops:
  0.6 34.8 %copy-start.7 = (bf16[128,2048]{1,0:T(8,128)(2,1)S(1)}, bf16[128,2048]{1,0:T(8,128)(2,1)}, u32[]{:S(2)}) copy-start(bf16[128,2048]{1,0:T(8,128)(2,1)} %param.12) | copy-start | bytes 1572868
  2.5 33.8 %copy-start = (bf16[272,1024]{1,0:T(8,128)(2,1)}, bf16[272,1024]{1,0:T(8,128)(2,1)S(1)}, u32[]{:S(2)}) copy-start(bf16[272,1024]{1,0:T(8,128)(2,1)S(1)} %fusion.2.rest_5_) | copy-start | bytes 1671172
  2.5 16.3 %collective-permute-start.1 = (bf16[272,1024]{1,0:T(8,128)(2,1)S(1)}, bf16[272,1024]{1,0:T(8,128)(2,1)S(1)}, u32[]{:S(2)}, u32[]{:S(2)}) collective-permute-start(bf16[272,1024]{1,0:T(8,128)(2,1)S(1)} %fusion.2.rest_5_), channel_id=1, source_target_pairs={{0,4},{2,6},{4,8},{6,10},{8,12},{10,14},{1,5},{3,7},{5,9},{7,11},{... | collective-permute-start | bytes 1671176 | tf_op jit(solution)/shard_map/ppermute | solution.py:127
  18.7 17.6 %copy-start.3 = (bf16[272,1024]{1,0:T(8,128)(2,1)}, bf16[272,1024]{1,0:T(8,128)(2,1)S(1)}, u32[]{:S(2)}) copy-start(bf16[272,1024]{1,0:T(8,128)(2,1)S(1)} %collective-permute-done.1.rest_1_) | copy-start | bytes 1671172
  18.7 15.4 %collective-permute-start.3 = (bf16[272,1024]{1,0:T(8,128)(2,1)S(1)}, bf16[272,1024]{1,0:T(8,128)(2,1)S(1)}, u32[]{:S(2)}, u32[]{:S(2)}) collective-permute-start(bf16[272,1024]{1,0:T(8,128)(2,1)S(1)} %collective-permute-done.1.rest_1_), channel_id=1, source_target_pairs={{0,4},{2,6},{4,8},{6,10},{8,12},{10,14},{1,5},{3,7},{5,9},{7,11},{... | collective-permute-start | bytes 1671176 | tf_op jit(solution)/shard_map/ppermute | solution.py:127
  22.2 20.3 %collective-permute-start = (bf16[272,1024]{1,0:T(8,128)(2,1)S(1)}, bf16[272,1024]{1,0:T(8,128)(2,1)S(1)}, u32[]{:S(2)}, u32[]{:S(2)}) collective-permute-start(bf16[272,1024]{1,0:T(8,128)(2,1)S(1)} %fusion.2.rest_5_), channel_id=1, source_target_pairs={{0,2},{4,6},{8,10},{12,14},{1,3},{5,7},{9,11},{13,15},{16,18},{20,... | collective-permute-start | bytes 1671176 | tf_op jit(solution)/shard_map/ppermute | solution.py:127
  25.7 22.6 %collective-permute-start.2 = (bf16[272,1024]{1,0:T(8,128)(2,1)S(1)}, bf16[272,1024]{1,0:T(8,128)(2,1)S(1)}, u32[]{:S(2)}, u32[]{:S(2)}) collective-permute-start(bf16[272,1024]{1,0:T(8,128)(2,1)S(1)} %collective-permute-done.1.rest_1_), channel_id=1, source_target_pairs={{0,2},{4,6},{8,10},{12,14},{2,0},{6,4},{10,8},{14,12},{1,3},{5,7},... | collective-permute-start | bytes 1671176 | tf_op jit(solution)/shard_map/ppermute | solution.py:127
  34.1 2.2 %copy-start.4 = (bf16[272,1024]{1,0:T(8,128)(2,1)}, bf16[272,1024]{1,0:T(8,128)(2,1)S(1)}, u32[]{:S(2)}) copy-start(bf16[272,1024]{1,0:T(8,128)(2,1)S(1)} %collective-permute-done.3.rest_3_) | copy-start | bytes 1671172
  34.1 16.6 %collective-permute-start.4 = (bf16[272,1024]{1,0:T(8,128)(2,1)S(1)}, bf16[272,1024]{1,0:T(8,128)(2,1)}, u32[]{:S(2)}, u32[]{:S(2)}) collective-permute-start(bf16[272,1024]{1,0:T(8,128)(2,1)S(1)} %collective-permute-done.3.rest_3_), channel_id=1, source_target_pairs={{2,0},{6,4},{10,8},{14,12},{3,1},{7,5},{11,9},{15,13},{18,16},{22,... | collective-permute-start | bytes 1671176 | tf_op jit(solution)/shard_map/ppermute | solution.py:127
  35.4 5.2 %copy-start.8 = (s32[256]{0:T(256)S(1)}, s32[256]{0:T(256)}, u32[]{:S(2)}) copy-start(s32[256]{0:T(256)} %param.13) | copy-start | bytes 3076
  35.5 5.2 %copy-start.9 = (f32[4]{0:T(128)S(1)}, f32[4]{0:T(128)}, u32[]{:S(2)}) copy-start(f32[4]{0:T(128)} %param.14) | copy-start | bytes 52
  36.3 5.2 %all-to-all-start = ((bf16[128,2,1024]{2,0,1:T(8,128)(2,1)}), bf16[128,2,1024]{2,0,1:T(8,128)(2,1)S(1)}, u32[]{:S(2)}, u32[]{:S(2)}) async-start(bf16[128,2,1024]{2,0,1:T(8,128)(2,1)} %bitcast.11), calls=%async_computation | async-start | bytes 1048576 | tf_op jit(solution)/shard_map/all_to_all | solution.py:140
  42.5 8.2 %copy-start.5 = (bf16[272,1024]{1,0:T(8,128)(2,1)}, bf16[272,1024]{1,0:T(8,128)(2,1)S(1)}, u32[]{:S(2)}) copy-start(bf16[272,1024]{1,0:T(8,128)(2,1)S(1)} %collective-permute-done.rest_0_) | copy-start | bytes 1671172
  48.3 2.4 %copy-start.6 = (bf16[272,1024]{1,0:T(8,128)(2,1)}, bf16[272,1024]{1,0:T(8,128)(2,1)S(1)}, u32[]{:S(2)}) copy-start(bf16[272,1024]{1,0:T(8,128)(2,1)S(1)} %collective-permute-done.2.rest_2_) | copy-start | bytes 1671172
  67.6 15.4 %collective-permute-start.5 = (bf16[256,1024]{1,0:T(8,128)(2,1)}, bf16[256,1024]{1,0:T(8,128)(2,1)S(1)}, u32[]{:S(2)}, u32[]{:S(2)}) collective-permute-start(bf16[256,1024]{1,0:T(8,128)(2,1)} %get-tuple-element.26), channel_id=1, source_target_pairs={{0,2},{4,6},{8,10},{12,14},{1,3},{5,7},{9,11},{13,15},{16,18},{20,... | collective-permute-start | bytes 1572872 | tf_op jit(solution)/shard_map/ppermute | solution.py:127
  70.4 20.7 %collective-permute-start.7 = (bf16[256,1024]{1,0:T(8,128)(2,1)}, bf16[256,1024]{1,0:T(8,128)(2,1)S(1)}, u32[]{:S(2)}, u32[]{:S(2)}) collective-permute-start(bf16[256,1024]{1,0:T(8,128)(2,1)} %get-tuple-element.27), channel_id=1, source_target_pairs={{0,2},{4,6},{8,10},{12,14},{2,0},{6,4},{10,8},{14,12},{1,3},{5,7},... | collective-permute-start | bytes 1572872 | tf_op jit(solution)/shard_map/ppermute | solution.py:127
  82.9 3.9 %copy-start.10 = (bf16[256,1024]{1,0:T(8,128)(2,1)S(1)}, bf16[256,1024]{1,0:T(8,128)(2,1)}, u32[]{:S(2)}) copy-start(bf16[256,1024]{1,0:T(8,128)(2,1)} %get-tuple-element.28) | copy-start | bytes 1572868
  83.0 15.0 %copy-start.2 = (f32[256,1024]{1,0:T(8,128)S(1)}, f32[256,1024]{1,0:T(8,128)}, u32[]{:S(2)}) copy-start(f32[256,1024]{1,0:T(8,128)} %get-tuple-element.24) | copy-start | bytes 3145732
  84.4 13.5 %collective-permute-start.6 = (bf16[256,1024]{1,0:T(8,128)(2,1)S(1)}, bf16[256,1024]{1,0:T(8,128)(2,1)S(1)}, u32[]{:S(2)}, u32[]{:S(2)}) collective-permute-start(bf16[256,1024]{1,0:T(8,128)(2,1)S(1)} %add_convert_fusion.2), channel_id=1, source_target_pairs={{4,0},{6,2},{8,4},{10,6},{12,8},{14,10},{5,1},{7,3},{9,5},{11,7},{... | collective-permute-start | bytes 1572872 | tf_op jit(solution)/shard_map/ppermute | solution.py:127
  86.9 13.9 %collective-permute-start.9 = (bf16[256,1024]{1,0:T(8,128)(2,1)S(1)}, bf16[256,1024]{1,0:T(8,128)(2,1)S(1)}, u32[]{:S(2)}, u32[]{:S(2)}) collective-permute-start(bf16[256,1024]{1,0:T(8,128)(2,1)S(1)} %copy-done.10), channel_id=1, source_target_pairs={{2,0},{6,4},{10,8},{14,12},{3,1},{7,5},{11,9},{15,13},{18,16},{22,... | collective-permute-start | bytes 1572872 | tf_op jit(solution)/shard_map/ppermute | solution.py:127
  97.9 11.5 %copy-start.1 = (f32[256,1024]{1,0:T(8,128)S(1)}, f32[256,1024]{1,0:T(8,128)}, u32[]{:S(2)}) copy-start(f32[256,1024]{1,0:T(8,128)} %get-tuple-element.23) | copy-start | bytes 3145732
  98.2 11.2 %collective-permute-start.8 = (bf16[256,1024]{1,0:T(8,128)(2,1)S(1)}, bf16[256,1024]{1,0:T(8,128)(2,1)S(1)}, u32[]{:S(2)}, u32[]{:S(2)}) collective-permute-start(bf16[256,1024]{1,0:T(8,128)(2,1)S(1)} %add_convert_fusion.1), channel_id=1, source_target_pairs={{4,0},{6,2},{8,4},{10,6},{12,8},{14,10},{5,1},{7,3},{9,5},{11,7},{... | collective-permute-start | bytes 1572872 | tf_op jit(solution)/shard_map/ppermute | solution.py:127
where the time goes:
time: 112 us; the launch traced here: 110 us
  waiting for transfers between devices  61 us (54%)
  starting transfers between devices  24.4 us (22%)
  Pallas kernels  16.8 us (15%)
  other arithmetic  4.83 us (4%)
  local copies, waits for them, and re-layouts  2.51 us (2%)
    ppermute x10, waiting for transfers between devices, permuted(): lax.ppermute(value, axis, [pair for pair in pairs if 0 <= pair[1] < lax.a...  60.2 us
    ppermute x10, starting transfers between devices, permuted(): lax.ppermute(value, axis, [pair for pair in pairs if 0 <= pair[1] < lax.a...  20.9 us
    pallas_call x1, Pallas kernels, head_group_grads(): pl.pallas_call(kernel, out_shape=out_shape, in_specs=[smem, smem] + [vmem...  16.8 us
    all_to_all x1, starting transfers between devices, device_body(): lax.all_to_all(grad_out, 'tsp', split_axis=1, concat_axis=0, tiled=True)  3.5 us
  transfers between devices with their start and end apart: 11, of which 9 were waited for; matrix products, arithmetic and copies ran while one was open for 4% of the time, Pallas kernels for 0%

commit v1 on v0

--- a/solution.py
+++ b/solution.py
@@ -9,6 +9,7 @@
 HEAD_DIMENSION = 128
 WINDOW = 1024
 ID_ROWS = 16
+CHUNK_HEADS = (2, 2)
 score_scale = 168.0 ** (-0.5)
 
 
@@ -24,7 +25,7 @@
     return lax.dot_general(a, b, (((1,), (0,)), ((), ())), preferred_element_type=jnp.float32)
 
 
-def attention_kernel(win_ref, odd_ref, qid_ref, q_ref, g_ref, *rest, group_size):
+def attention_kernel(win_ref, odd_ref, qid_ref, q_ref, g_ref, *rest, group_size, first_head):
     r1, r2, r3, r4, r5, own = rest[:6]
     dq_ref, p4_ref, p2_ref, p1_ref, p3_ref, b3_ref, own_ref = rest[6:]
     d = HEAD_DIMENSION
@@ -57,7 +58,8 @@
     for kv in range(width // d):
         keys = [src((slice(0, rows), slice(kv * d, (kv + 1) * d))) for src in sources]
         values = [src((slice(0, rows), slice(width + kv * d, width + (kv + 1) * d))) for src in sources]
-        parts = kv_head(win_ref, q_ref, g_ref, dq_ref, keys, values, offset, base_live, kv, group_size)
+        parts = kv_head(win_ref, q_ref, g_ref, dq_ref, keys, values, offset, base_live, kv, group_size,
+                        first_head)
         kcols = slice(kv * d, (kv + 1) * d)
         vcols = slice(width + kv * d, width + (kv + 1) * d)
         for target, p in ((p4_ref, 0), (p2_ref, 2), (p1_ref, 3), (p3_ref, 1)):
@@ -69,7 +71,8 @@
         own_ref[:, vcols] = parts[4][1]
 
 
-def kv_head(win_ref, q_ref, g_ref, dq_ref, keys, values, offset, base_live, kv, group_size):
+def kv_head(win_ref, q_ref, g_ref, dq_ref, keys, values, offset, base_live, kv, group_size,
+            first_head):
     d = HEAD_DIMENSION
     pieces = len(keys)
     piece_rows = q_ref.shape[0]
@@ -77,10 +80,11 @@
     value_acc = [jnp.zeros((piece_rows, d), jnp.float32) for _ in range(pieces)]
     for h in range(group_size):
         head = kv * group_size + h
-        query = q_ref[:, head * d : (head + 1) * d]
-        grad = g_ref[:, head * d : (head + 1) * d]
+        column = (first_head + head) * d
+        query = q_ref[:, column : column + d]
+        grad = g_ref[:, column : column + d]
         scores = jnp.concatenate([_nt(query, key) for key in keys], axis=1) * score_scale
-        live = base_live & (offset < win_ref[head])
+        live = base_live & (offset < win_ref[first_head + head])
         scores = jnp.where(live, scores, jnp.float32(-1e30))
         top = jnp.max(scores, axis=1, keepdims=True)
         prob = jnp.exp(scores - top)
@@ -104,16 +108,16 @@
     return [(key_acc[p] * score_scale, value_acc[p]) for p in range(pieces)]
 
 
-def head_group_grads(windows, odd, query_ids, query, grad, payloads):
+def head_group_grads(windows, odd, query_ids, query, grad, payloads, group_size, first_head):
     rows = query.shape[0]
     pair_width = payloads[0].shape[1]
-    group_size = 2 * query.shape[1] // pair_width
     vmem = pl.BlockSpec(memory_space=pltpu.VMEM)
     smem = pl.BlockSpec(memory_space=pltpu.SMEM)
     wide = jax.ShapeDtypeStruct((rows, pair_width), jnp.float32)
     low = jax.ShapeDtypeStruct((rows, pair_width), jnp.bfloat16)
-    out_shape = [jax.ShapeDtypeStruct(query.shape, jnp.bfloat16), wide, wide, low, low, low, wide]
-    kernel = functools.partial(attention_kernel, group_size=group_size)
+    dq_shape = jax.ShapeDtypeStruct((rows, group_size * pair_width // 2), jnp.bfloat16)
+    out_shape = [dq_shape, wide, wide, low, low, low, wide]
+    kernel = functools.partial(attention_kernel, group_size=group_size, first_head=first_head)
     return pl.pallas_call(
         kernel,
         out_shape=out_shape,
@@ -141,34 +145,50 @@
     weighted = (token_weight[:, None] * grad_local.astype(jnp.float32)).astype(jnp.bfloat16)
     query_ids = (doc_ids + 1).astype(jnp.float32)[:, None]
 
-    paired = jnp.concatenate([key_proj, value_projection], axis=1)
-    id_rows = jnp.zeros((ID_ROWS, 2 * kv_width), jnp.bfloat16)
-    id_rows = id_rows.at[0, :tok_rows].set((doc_ids + 1).astype(jnp.bfloat16))
-    payload = jnp.concatenate([paired, id_rows], axis=0)
-
+    kv_heads = kv_width // HEAD_DIMENSION
+    group_size = query_proj.shape[1] // kv_width
     evens = range(0, count, 2)
     odds = range(1, count, 2)
     everyone = range(count)
     swap = [(c, c + 1) for c in evens] + [(c, c - 1) for c in odds]
-    got1 = permuted(payload, "ctx", [(c, c + 1) for c in evens])
-    got2 = permuted(payload, "ctx", [(c, c + 2) for c in everyone])
-    got3 = permuted(got2, "ctx", swap)
-    got4 = permuted(got2, "ctx", [(c, c + 2) for c in everyone])
-    got5 = permuted(got4, "ctx", [(c, c - 1) for c in odds])
-
-    query_grad, part4, part2, part1, part3, back3, own_part = head_group_grads(
-        head_window, odd, query_ids, query_proj, weighted, [got1, got2, got3, got4, got5, payload]
-    )
-    from5 = permuted(part3, "ctx", [(c, c + 1) for c in evens])
-    from3 = permuted(back3, "ctx", swap)
-    from1 = permuted(part1, "ctx", [(c, c - 1) for c in odds])
-    send4 = (part4 + from5.astype(jnp.float32)).astype(jnp.bfloat16)
-    from4 = permuted(send4, "ctx", [(c, c - 2) for c in everyone])
-    send2 = (part2 + from4.astype(jnp.float32) + from3.astype(jnp.float32)).astype(jnp.bfloat16)
-    from2 = permuted(send2, "ctx", [(c, c - 2) for c in everyone])
-    summed = own_part + from2.astype(jnp.float32) + from1.astype(jnp.float32)
-    key_grad = summed[:, :kv_width].astype(jnp.bfloat16)
-    value_grad = summed[:, kv_width:].astype(jnp.bfloat16)
+    chunk_sizes = CHUNK_HEADS if sum(CHUNK_HEADS) == kv_heads else (kv_heads,)
+    query_pieces, key_pieces, value_pieces = [], [], []
+    previous = None
+    chunk_first = 0
+    for chunk_heads in chunk_sizes:
+        width = chunk_heads * HEAD_DIMENSION
+        cols = slice(chunk_first * HEAD_DIMENSION, chunk_first * HEAD_DIMENSION + width)
+        paired = jnp.concatenate([key_proj[:, cols], value_projection[:, cols]], axis=1)
+        id_rows = jnp.zeros((ID_ROWS, 2 * width), jnp.bfloat16)
+        id_rows = id_rows.at[0, :tok_rows].set((doc_ids + 1).astype(jnp.bfloat16))
+        payload = jnp.concatenate([paired, id_rows], axis=0)
+        if previous is not None:
+            payload, _ = lax.optimization_barrier((payload, previous))
+        got1 = permuted(payload, "ctx", [(c, c + 1) for c in evens])
+        got2 = permuted(payload, "ctx", [(c, c + 2) for c in everyone])
+        got3 = permuted(got2, "ctx", swap)
+        got4 = permuted(got2, "ctx", [(c, c + 2) for c in everyone])
+        got5 = permuted(got4, "ctx", [(c, c - 1) for c in odds])
+        previous = (got1, got3, got5)
+        query_part, part4, part2, part1, part3, back3, own_part = head_group_grads(
+            head_window, odd, query_ids, query_proj, weighted,
+            [got1, got2, got3, got4, got5, payload], group_size, chunk_first * group_size,
+        )
+        chunk_first += chunk_heads
+        from5 = permuted(part3, "ctx", [(c, c + 1) for c in evens])
+        from3 = permuted(back3, "ctx", swap)
+        from1 = permuted(part1, "ctx", [(c, c - 1) for c in odds])
+        send4 = (part4 + from5.astype(jnp.float32)).astype(jnp.bfloat16)
+        from4 = permuted(send4, "ctx", [(c, c - 2) for c in everyone])
+        send2 = (part2 + from4.astype(jnp.float32) + from3.astype(jnp.float32)).astype(jnp.bfloat16)
+        from2 = permuted(send2, "ctx", [(c, c - 2) for c in everyone])
+        summed = own_part + from2.astype(jnp.float32) + from1.astype(jnp.float32)
+        query_pieces.append(query_part)
+        key_pieces.append(summed[:, :width])
+        value_pieces.append(summed[:, width:])
+    query_grad = jnp.concatenate(query_pieces, axis=1)
+    key_grad = jnp.concatenate(key_pieces, axis=1).astype(jnp.bfloat16)
+    value_grad = jnp.concatenate(value_pieces, axis=1).astype(jnp.bfloat16)
     return (query_grad, key_grad, value_grad)
 
 

time: 112 us -> 124 us (1.11)
  the two profiles are of different devices: /device:TPU:8 before, /device:TPU:0 now
where the time goes in v1:
time: 124 us; the launch traced here: 123 us
  waiting for transfers between devices  48 us (39%)
  starting transfers between devices  44.8 us (36%)
  Pallas kernels  18.1 us (15%)
  other arithmetic  5.73 us (5%)
  local copies, waits for them, and re-layouts  5.15 us (4%)
    ppermute x20, waiting for transfers between devices, permuted(): lax.ppermute(value, axis, [pair for pair in pairs if 0 <= pair[1] < lax.a...  48 us
    ppermute x20, starting transfers between devices, permuted(): lax.ppermute(value, axis, [pair for pair in pairs if 0 <= pair[1] < lax.a...  41.3 us
    pallas_call x2, Pallas kernels, head_group_grads(): pl.pallas_call(kernel, out_shape=out_shape, in_specs=[smem, smem] + [vmem...  18.1 us
    all_to_all x1, starting transfers between devices, device_body(): lax.all_to_all(grad_out, 'tsp', split_axis=1, concat_axis=0, tiled=True)  3.5 us
  transfers between devices with their start and end apart: 21, of which 13 were waited for; matrix products, arithmetic and copies ran while one was open for 4% of the time, Pallas kernels for 15%

profile of v1, /device:TPU:0, one launch (start us, length us, event | category | flops | bytes accessed | tf_op | source)
XLA Modules:
  0.0 122.9 jit_solution(3477924789033930968)
XLA Ops:
  0.6 0.7 add_convert_fusion.6
  1.3 1.1 fusion.6
  2.5 0.0 copy-start.2
  2.5 5.1 %collective-permute-start.1 = (bf16[272,512]{1,0:T(8,128)(2,1)S(1)}, bf16[272,512]{1,0:T(8,128)(2,1)S(1)}, u32[]{:S(2)}, u32[]{:S(2)}) collective-permute-start(bf16[272,512]{1,0:T(8,128)(2,1)S(1)} %get-tuple-element.61.rest_5_), channel_id=1, source_target_pairs={{0,4},{2,6},{4,8},{6,10},{8,12},{10,14},{1,5},{3,7},{5,9},{7,11},{... | collective-permute-start | bytes 835592 | tf_op jit(solution)/shard_map/ppermute | solution.py:131
  7.6 5.9 %collective-permute-done.1.rest_1_ = bf16[272,512]{1,0:T(8,128)(2,1)S(1)} collective-permute-done((bf16[272,512]{1,0:T(8,128)(2,1)S(1)}, bf16[272,512]{1,0:T(8,128)(2,1)S(1)}, u32[]{:S(2)}, u32[]{:S(2)}) %collective-permute-start.1) | collective-permute-done | bytes 278560 | tf_op jit(solution)/shard_map/ppermute | solution.py:131
  13.5 4.4 %collective-permute-start.3 = (bf16[272,512]{1,0:T(8,128)(2,1)S(1)}, bf16[272,512]{1,0:T(8,128)(2,1)S(1)}, u32[]{:S(2)}, u32[]{:S(2)}) collective-permute-start(bf16[272,512]{1,0:T(8,128)(2,1)S(1)} %collective-permute-done.1.rest_1_), channel_id=1, source_target_pairs={{0,4},{2,6},{4,8},{6,10},{8,12},{10,14},{1,5},{3,7},{5,9},{7,11},{... | collective-permute-start | bytes 835592 | tf_op jit(solution)/shard_map/ppermute | solution.py:131
  17.9 3.4 %collective-permute-start = (bf16[272,512]{1,0:T(8,128)(2,1)S(1)}, bf16[272,512]{1,0:T(8,128)(2,1)S(1)}, u32[]{:S(2)}, u32[]{:S(2)}) collective-permute-start(bf16[272,512]{1,0:T(8,128)(2,1)S(1)} %get-tuple-element.61.rest_5_), channel_id=1, source_target_pairs={{0,2},{4,6},{8,10},{12,14},{1,3},{5,7},{9,11},{13,15},{16,18},{20,... | collective-permute-start | bytes 835592 | tf_op jit(solution)/shard_map/ppermute | solution.py:131
  21.3 0.1 collective-permute-start.2
  21.4 1.5 %collective-permute-done.3.rest_3_ = bf16[272,512]{1,0:T(8,128)(2,1)S(1)} collective-permute-done((bf16[272,512]{1,0:T(8,128)(2,1)S(1)}, bf16[272,512]{1,0:T(8,128)(2,1)S(1)}, u32[]{:S(2)}, u32[]{:S(2)}) %collective-permute-start.3) | collective-permute-done | bytes 278560 | tf_op jit(solution)/shard_map/ppermute | solution.py:131
  23.0 1.3 %collective-permute-start.4 = (bf16[272,512]{1,0:T(8,128)(2,1)S(1)}, bf16[272,512]{1,0:T(8,128)(2,1)S(1)}, u32[]{:S(2)}, u32[]{:S(2)}) collective-permute-start(bf16[272,512]{1,0:T(8,128)(2,1)S(1)} %collective-permute-done.3.rest_3_), channel_id=1, source_target_pairs={{2,0},{6,4},{10,8},{14,12},{3,1},{7,5},{11,9},{15,13},{18,16},{22,... | collective-permute-start | bytes 835592 | tf_op jit(solution)/shard_map/ppermute | solution.py:131
  24.2 4.1 %collective-permute-done.rest_0_ = bf16[272,512]{1,0:T(8,128)(2,1)S(1)} collective-permute-done((bf16[272,512]{1,0:T(8,128)(2,1)S(1)}, bf16[272,512]{1,0:T(8,128)(2,1)S(1)}, u32[]{:S(2)}, u32[]{:S(2)}) %collective-permute-start) | collective-permute-done | bytes 278560 | tf_op jit(solution)/shard_map/ppermute | solution.py:131
  28.4 3.7 %collective-permute-done.2.rest_2_ = bf16[272,512]{1,0:T(8,128)(2,1)S(1)} collective-permute-done((bf16[272,512]{1,0:T(8,128)(2,1)S(1)}, bf16[272,512]{1,0:T(8,128)(2,1)S(1)}, u32[]{:S(2)}, u32[]{:S(2)}) %collective-permute-start.2) | collective-permute-done | bytes 278560 | tf_op jit(solution)/shard_map/ppermute | solution.py:131
  32.1 2.3 %collective-permute-done.4.rest_4_ = bf16[272,512]{1,0:T(8,128)(2,1)S(1)} collective-permute-done((bf16[272,512]{1,0:T(8,128)(2,1)S(1)}, bf16[272,512]{1,0:T(8,128)(2,1)S(1)}, u32[]{:S(2)}, u32[]{:S(2)}) %collective-permute-start.4) | collective-permute-done | bytes 278560 | tf_op jit(solution)/shard_map/ppermute | solution.py:131
  34.4 3.5 %collective-permute-start.6 = (bf16[272,512]{1,0:T(8,128)(2,1)S(1)}, bf16[272,512]{1,0:T(8,128)(2,1)S(1)}, u32[]{:S(2)}, u32[]{:S(2)}) collective-permute-start(bf16[272,512]{1,0:T(8,128)(2,1)S(1)} %get-tuple-element.39.rest_5_), channel_id=1, source_target_pairs={{0,4},{2,6},{4,8},{6,10},{8,12},{10,14},{1,5},{3,7},{5,9},{7,11},{... | collective-permute-start | bytes 835592 | tf_op jit(solution)/shard_map/ppermute | solution.py:131
  37.9 0.8 copy.19
  38.7 3.5 %all-to-all-start = ((bf16[128,2,1024]{2,0,1:T(8,128)(2,1)}), bf16[128,2,1024]{2,0,1:T(8,128)(2,1)S(1)}, u32[]{:S(2)}, u32[]{:S(2)}) async-start(bf16[128,2,1024]{2,0,1:T(8,128)(2,1)} %bitcast.11), calls=%async_computation | async-start | bytes 1048576 | tf_op jit(solution)/shard_map/all_to_all | solution.py:144
  42.3 0.1 select_reduce_fusion
  42.4 0.0 collective-permute-done.6.rest_1_
  42.4 4.1 %collective-permute-start.8 = (bf16[272,512]{1,0:T(8,128)(2,1)S(1)}, bf16[272,512]{1,0:T(8,128)(2,1)S(1)}, u32[]{:S(2)}, u32[]{:S(2)}) collective-permute-start(bf16[272,512]{1,0:T(8,128)(2,1)S(1)} %collective-permute-done.6.rest_1_), channel_id=1, source_target_pairs={{0,4},{2,6},{4,8},{6,10},{8,12},{10,14},{1,5},{3,7},{5,9},{7,11},{... | collective-permute-start | bytes 835592 | tf_op jit(solution)/shard_map/ppermute | solution.py:131
  46.5 0.0 all-to-all-done
  46.5 0.9 fusion.g_ref
  47.4 0.8 copy.15.qid_ref
  48.2 9.0 %attention_group.2 = (bf16[256,512]{1,0:T(8,128)(2,1)}, f32[256,512]{1,0:T(8,128)}, f32[256,512]{1,0:T(8,128)}, bf16[256,512]{1,0:T(8,128)(2,1)}, bf16[256,512]{...) custom-call(s32[8]{0:T(128)} %win_ref.3, s32[1]{0:T(128)} %bitcast.odd_ref, f32[256,1]{1,0:T(8,128)} %copy.15.qid_ref, ...), custom_call_target="tpu_custom_call" | custom-call | tf_op jit(solution)/shard_map/attention_group/pallas_call | solution.py:121
  57.3 1.9 %collective-permute-start.10 = (bf16[256,512]{1,0:T(8,128)(2,1)}, bf16[256,512]{1,0:T(8,128)(2,1)S(1)}, u32[]{:S(2)}, u32[]{:S(2)}) collective-permute-start(bf16[256,512]{1,0:T(8,128)(2,1)} %get-tuple-element.44), channel_id=1, source_target_pairs={{0,2},{4,6},{8,10},{12,14},{1,3},{5,7},{9,11},{13,15},{16,18},{20,... | collective-permute-start | bytes 786440 | tf_op jit(solution)/shard_map/ppermute | solution.py:131
  59.2 1.3 %collective-permute-start.5 = (bf16[272,512]{1,0:T(8,128)(2,1)S(1)}, bf16[272,512]{1,0:T(8,128)(2,1)S(1)}, u32[]{:S(2)}, u32[]{:S(2)}) collective-permute-start(bf16[272,512]{1,0:T(8,128)(2,1)S(1)} %get-tuple-element.39.rest_5_), channel_id=1, source_target_pairs={{0,2},{4,6},{8,10},{12,14},{1,3},{5,7},{9,11},{13,15},{16,18},{20,... | collective-permute-start | bytes 835592 | tf_op jit(solution)/shard_map/ppermute | solution.py:131
  60.5 0.1 collective-permute-start.12
  60.6 2.0 %collective-permute-start.7 = (bf16[272,512]{1,0:T(8,128)(2,1)S(1)}, bf16[272,512]{1,0:T(8,128)(2,1)S(1)}, u32[]{:S(2)}, u32[]{:S(2)}) collective-permute-start(bf16[272,512]{1,0:T(8,128)(2,1)S(1)} %collective-permute-done.6.rest_1_), channel_id=1, source_target_pairs={{0,2},{4,6},{8,10},{12,14},{2,0},{6,4},{10,8},{14,12},{1,3},{5,7},... | collective-permute-start | bytes 835592 | tf_op jit(solution)/shard_map/ppermute | solution.py:131
  62.6 0.0 collective-permute-done.8.rest_3_
  62.6 1.3 %collective-permute-start.9 = (bf16[272,512]{1,0:T(8,128)(2,1)S(1)}, bf16[272,512]{1,0:T(8,128)(2,1)S(1)}, u32[]{:S(2)}, u32[]{:S(2)}) collective-permute-start(bf16[272,512]{1,0:T(8,128)(2,1)S(1)} %collective-permute-done.8.rest_3_), channel_id=1, source_target_pairs={{2,0},{6,4},{10,8},{14,12},{3,1},{7,5},{11,9},{15,13},{18,16},{22,... | collective-permute-start | bytes 835592 | tf_op jit(solution)/shard_map/ppermute | solution.py:131
  63.9 2.3 %collective-permute-done.10 = bf16[256,512]{1,0:T(8,128)(2,1)S(1)} collective-permute-done((bf16[256,512]{1,0:T(8,128)(2,1)}, bf16[256,512]{1,0:T(8,128)(2,1)S(1)}, u32[]{:S(2)}, u32[]{:S(2)}) %collective-permute-start.10) | collective-permute-done | bytes 262176 | tf_op jit(solution)/shard_map/ppermute | solution.py:131
  66.1 1.2 add_convert_fusion.5
  67.3 1.3 %collective-permute-start.11 = (bf16[256,512]{1,0:T(8,128)(2,1)S(1)}, bf16[256,512]{1,0:T(8,128)(2,1)S(1)}, u32[]{:S(2)}, u32[]{:S(2)}) collective-permute-start(bf16[256,512]{1,0:T(8,128)(2,1)S(1)} %add_convert_fusion.5), channel_id=1, source_target_pairs={{4,0},{6,2},{8,4},{10,6},{12,8},{14,10},{5,1},{7,3},{9,5},{11,7},{... | collective-permute-start | bytes 786440 | tf_op jit(solution)/shard_map/ppermute | solution.py:131
  68.6 3.4 %collective-permute-done.5.rest_0_ = bf16[272,512]{1,0:T(8,128)(2,1)S(1)} collective-permute-done((bf16[272,512]{1,0:T(8,128)(2,1)S(1)}, bf16[272,512]{1,0:T(8,128)(2,1)S(1)}, u32[]{:S(2)}, u32[]{:S(2)}) %collective-permute-start.5) | collective-permute-done | bytes 278560 | tf_op jit(solution)/shard_map/ppermute | solution.py:131
  72.0 1.6 %collective-permute-start.14 = (bf16[256,512]{1,0:T(8,128)(2,1)S(1)}, bf16[256,512]{1,0:T(8,128)(2,1)S(1)}, u32[]{:S(2)}, u32[]{:S(2)}) collective-permute-start(bf16[256,512]{1,0:T(8,128)(2,1)S(1)} %copy-done.22), channel_id=1, source_target_pairs={{2,0},{6,4},{10,8},{14,12},{3,1},{7,5},{11,9},{15,13},{18,16},{22,... | collective-permute-start | bytes 786440 | tf_op jit(solution)/shard_map/ppermute | solution.py:131
  73.6 8.8 %collective-permute-done.7.rest_2_ = bf16[272,512]{1,0:T(8,128)(2,1)S(1)} collective-permute-done((bf16[272,512]{1,0:T(8,128)(2,1)S(1)}, bf16[272,512]{1,0:T(8,128)(2,1)S(1)}, u32[]{:S(2)}, u32[]{:S(2)}) %collective-permute-start.7) | collective-permute-done | bytes 278560 | tf_op jit(solution)/shard_map/ppermute | solution.py:131
  82.4 0.0 collective-permute-done.9.rest_4_
  82.4 0.7 copy-done.16
  83.1 0.7 copy-done.17
  83.9 9.1 %attention_group.3 = (bf16[256,512]{1,0:T(8,128)(2,1)}, f32[256,512]{1,0:T(8,128)}, f32[256,512]{1,0:T(8,128)}, bf16[256,512]{1,0:T(8,128)(2,1)}, bf16[256,512]{...) custom-call(s32[8]{0:T(128)} %win_ref.3, s32[1]{0:T(128)} %bitcast.odd_ref, f32[256,1]{1,0:T(8,128)} %copy.15.qid_ref, ...), custom_call_target="tpu_custom_call" | custom-call | tf_op jit(solution)/shard_map/attention_group/pallas_call | solution.py:121
  92.9 4.4 %collective-permute-start.15 = (bf16[256,512]{1,0:T(8,128)(2,1)}, bf16[256,512]{1,0:T(8,128)(2,1)S(1)}, u32[]{:S(2)}, u32[]{:S(2)}) collective-permute-start(bf16[256,512]{1,0:T(8,128)(2,1)} %get-tuple-element.50), channel_id=1, source_target_pairs={{0,2},{4,6},{8,10},{12,14},{1,3},{5,7},{9,11},{13,15},{16,18},{20,... | collective-permute-start | bytes 786440 | tf_op jit(solution)/shard_map/ppermute | solution.py:131
  97.3 0.0 collective-permute-done.12
  97.3 0.0 collective-permute-done.11
  97.4 0.1 add_convert_fusion.4
  97.5 1.4 %collective-permute-start.13 = (bf16[256,512]{1,0:T(8,128)(2,1)S(1)}, bf16[256,512]{1,0:T(8,128)(2,1)S(1)}, u32[]{:S(2)}, u32[]{:S(2)}) collective-permute-start(bf16[256,512]{1,0:T(8,128)(2,1)S(1)} %add_convert_fusion.4), channel_id=1, source_target_pairs={{4,0},{6,2},{8,4},{10,6},{12,8},{14,10},{5,1},{7,3},{9,5},{11,7},{... | collective-permute-start | bytes 786440 | tf_op jit(solution)/shard_map/ppermute | solution.py:131
  98.9 0.1 collective-permute-start.17
  99.0 5.3 %collective-permute-done.15 = bf16[256,512]{1,0:T(8,128)(2,1)S(1)} collective-permute-done((bf16[256,512]{1,0:T(8,128)(2,1)}, bf16[256,512]{1,0:T(8,128)(2,1)S(1)}, u32[]{:S(2)}, u32[]{:S(2)}) %collective-permute-start.15) | collective-permute-done | bytes 262176 | tf_op jit(solution)/shard_map/ppermute | solution.py:131
  104.3 0.1 add_convert_fusion.2
  104.4 1.4 %collective-permute-start.16 = (bf16[256,512]{1,0:T(8,128)(2,1)S(1)}, bf16[256,512]{1,0:T(8,128)(2,1)S(1)}, u32[]{:S(2)}, u32[]{:S(2)}) collective-permute-start(bf16[256,512]{1,0:T(8,128)(2,1)S(1)} %add_convert_fusion.2), channel_id=1, source_target_pairs={{4,0},{6,2},{8,4},{10,6},{12,8},{14,10},{5,1},{7,3},{9,5},{11,7},{... | collective-permute-start | bytes 786440 | tf_op jit(solution)/shard_map/ppermute | solution.py:131
  105.8 0.0 collective-permute-done.14
  105.8 1.9 %collective-permute-done.13 = bf16[256,512]{1,0:T(8,128)(2,1)S(1)} collective-permute-done((bf16[256,512]{1,0:T(8,128)(2,1)S(1)}, bf16[256,512]{1,0:T(8,128)(2,1)S(1)}, u32[]{:S(2)}, u32[]{:S(2)}) %collective-permute-start.13) | collective-permute-done | bytes 262176 | tf_op jit(solution)/shard_map/ppermute | solution.py:131
  107.7 0.1 add_convert_fusion.3
  107.8 0.8 copy-done.23
  108.7 1.3 %collective-permute-start.19 = (bf16[256,512]{1,0:T(8,128)(2,1)S(1)}, bf16[256,512]{1,0:T(8,128)(2,1)S(1)}, u32[]{:S(2)}, u32[]{:S(2)}) collective-permute-start(bf16[256,512]{1,0:T(8,128)(2,1)S(1)} %copy-done.23), channel_id=1, source_target_pairs={{2,0},{6,4},{10,8},{14,12},{3,1},{7,5},{11,9},{15,13},{18,16},{22,... | collective-permute-start | bytes 786440 | tf_op jit(solution)/shard_map/ppermute | solution.py:131
  109.9 0.0 collective-permute-done.17
  110.0 2.8 %collective-permute-done.16 = bf16[256,512]{1,0:T(8,128)(2,1)S(1)} collective-permute-done((bf16[256,512]{1,0:T(8,128)(2,1)S(1)}, bf16[256,512]{1,0:T(8,128)(2,1)S(1)}, u32[]{:S(2)}, u32[]{:S(2)}) %collective-permute-start.16) | collective-permute-done | bytes 262176 | tf_op jit(solution)/shard_map/ppermute | solution.py:131
  112.8 0.1 add_convert_fusion.1
  112.9 0.0 copy-start.19
  112.9 1.4 %collective-permute-start.18 = (bf16[256,512]{1,0:T(8,128)(2,1)S(1)}, bf16[256,512]{1,0:T(8,128)(2,1)S(1)}, u32[]{:S(2)}, u32[]{:S(2)}) collective-permute-start(bf16[256,512]{1,0:T(8,128)(2,1)S(1)} %add_convert_fusion.1), channel_id=1, source_target_pairs={{4,0},{6,2},{8,4},{10,6},{12,8},{14,10},{5,1},{7,3},{9,5},{11,7},{... | collective-permute-start | bytes 786440 | tf_op jit(solution)/shard_map/ppermute | solution.py:131
  114.4 0.9 pad_maximum_fusion
  115.3 1.6 %collective-permute-done.19 = bf16[256,512]{1,0:T(8,128)(2,1)S(1)} collective-permute-done((bf16[256,512]{1,0:T(8,128)(2,1)S(1)}, bf16[256,512]{1,0:T(8,128)(2,1)S(1)}, u32[]{:S(2)}, u32[]{:S(2)}) %collective-permute-start.19) | collective-permute-done | bytes 262176 | tf_op jit(solution)/shard_map/ppermute | solution.py:131
  116.9 4.4 %collective-permute-done.18 = bf16[256,512]{1,0:T(8,128)(2,1)S(1)} collective-permute-done((bf16[256,512]{1,0:T(8,128)(2,1)S(1)}, bf16[256,512]{1,0:T(8,128)(2,1)S(1)}, u32[]{:S(2)}, u32[]{:S(2)}) %collective-permute-start.18) | collective-permute-done | bytes 262176 | tf_op jit(solution)/shard_map/ppermute | solution.py:131
  121.3 0.1 add_convert_fusion
  121.4 0.7 pad_maximum_fusion.2
  122.2 0.7 pad_maximum_fusion.1
  (49 shorter events, 0.2 us)
Async XLA Ops:
  2.5 35.4 %copy-start.2 = (bf16[128,2048]{1,0:T(8,128)(2,1)S(1)}, bf16[128,2048]{1,0:T(8,128)(2,1)}, u32[]{:S(2)}) copy-start(bf16[128,2048]{1,0:T(8,128)(2,1)} %param.14) | copy-start | bytes 1572868
  2.5 36.2 %copy-start.1 = (bf16[272,512]{1,0:T(8,128)(2,1)}, bf16[272,512]{1,0:T(8,128)(2,1)S(1)}, u32[]{:S(2)}) copy-start(bf16[272,512]{1,0:T(8,128)(2,1)S(1)} %get-tuple-element.61.rest_5_) | copy-start | bytes 835588
  2.5 56.6 %copy-start = (bf16[272,512]{1,0:T(8,128)(2,1)}, bf16[272,512]{1,0:T(8,128)(2,1)S(1)}, u32[]{:S(2)}) copy-start(bf16[272,512]{1,0:T(8,128)(2,1)S(1)} %get-tuple-element.39.rest_5_) | copy-start | bytes 835588
  2.5 11.0 %collective-permute-start.1 = (bf16[272,512]{1,0:T(8,128)(2,1)S(1)}, bf16[272,512]{1,0:T(8,128)(2,1)S(1)}, u32[]{:S(2)}, u32[]{:S(2)}) collective-permute-start(bf16[272,512]{1,0:T(8,128)(2,1)S(1)} %get-tuple-element.61.rest_5_), channel_id=1, source_target_pairs={{0,4},{2,6},{4,8},{6,10},{8,12},{10,14},{1,5},{3,7},{5,9},{7,11},{... | collective-permute-start | bytes 835592 | tf_op jit(solution)/shard_map/ppermute | solution.py:131
  13.5 25.2 %copy-start.10 = (bf16[272,512]{1,0:T(8,128)(2,1)}, bf16[272,512]{1,0:T(8,128)(2,1)S(1)}, u32[]{:S(2)}) copy-start(bf16[272,512]{1,0:T(8,128)(2,1)S(1)} %collective-permute-done.1.rest_1_) | copy-start | bytes 835588
  13.5 9.4 %collective-permute-start.3 = (bf16[272,512]{1,0:T(8,128)(2,1)S(1)}, bf16[272,512]{1,0:T(8,128)(2,1)S(1)}, u32[]{:S(2)}, u32[]{:S(2)}) collective-permute-start(bf16[272,512]{1,0:T(8,128)(2,1)S(1)} %collective-permute-done.1.rest_1_), channel_id=1, source_target_pairs={{0,4},{2,6},{4,8},{6,10},{8,12},{10,14},{1,5},{3,7},{5,9},{7,11},{... | collective-permute-start | bytes 835592 | tf_op jit(solution)/shard_map/ppermute | solution.py:131
  17.9 10.4 %collective-permute-start = (bf16[272,512]{1,0:T(8,128)(2,1)S(1)}, bf16[272,512]{1,0:T(8,128)(2,1)S(1)}, u32[]{:S(2)}, u32[]{:S(2)}) collective-permute-start(bf16[272,512]{1,0:T(8,128)(2,1)S(1)} %get-tuple-element.61.rest_5_), channel_id=1, source_target_pairs={{0,2},{4,6},{8,10},{12,14},{1,3},{5,7},{9,11},{13,15},{16,18},{20,... | collective-permute-start | bytes 835592 | tf_op jit(solution)/shard_map/ppermute | solution.py:131
  21.3 10.7 %collective-permute-start.2 = (bf16[272,512]{1,0:T(8,128)(2,1)S(1)}, bf16[272,512]{1,0:T(8,128)(2,1)S(1)}, u32[]{:S(2)}, u32[]{:S(2)}) collective-permute-start(bf16[272,512]{1,0:T(8,128)(2,1)S(1)} %collective-permute-done.1.rest_1_), channel_id=1, source_target_pairs={{0,2},{4,6},{8,10},{12,14},{2,0},{6,4},{10,8},{14,12},{1,3},{5,7},... | collective-permute-start | bytes 835592 | tf_op jit(solution)/shard_map/ppermute | solution.py:131
  23.0 15.8 %copy-start.11 = (bf16[272,512]{1,0:T(8,128)(2,1)}, bf16[272,512]{1,0:T(8,128)(2,1)S(1)}, u32[]{:S(2)}) copy-start(bf16[272,512]{1,0:T(8,128)(2,1)S(1)} %collective-permute-done.3.rest_3_) | copy-start | bytes 835588
  23.0 11.4 %collective-permute-start.4 = (bf16[272,512]{1,0:T(8,128)(2,1)S(1)}, bf16[272,512]{1,0:T(8,128)(2,1)S(1)}, u32[]{:S(2)}, u32[]{:S(2)}) collective-permute-start(bf16[272,512]{1,0:T(8,128)(2,1)S(1)} %collective-permute-done.3.rest_3_), channel_id=1, source_target_pairs={{2,0},{6,4},{10,8},{14,12},{3,1},{7,5},{11,9},{15,13},{18,16},{22,... | collective-permute-start | bytes 835592 | tf_op jit(solution)/shard_map/ppermute | solution.py:131
  28.4 10.4 %copy-start.12 = (bf16[272,512]{1,0:T(8,128)(2,1)}, bf16[272,512]{1,0:T(8,128)(2,1)S(1)}, u32[]{:S(2)}) copy-start(bf16[272,512]{1,0:T(8,128)(2,1)S(1)} %collective-permute-done.rest_0_) | copy-start | bytes 835588
  32.1 6.7 %copy-start.13 = (bf16[272,512]{1,0:T(8,128)(2,1)}, bf16[272,512]{1,0:T(8,128)(2,1)S(1)}, u32[]{:S(2)}) copy-start(bf16[272,512]{1,0:T(8,128)(2,1)S(1)} %collective-permute-done.2.rest_2_) | copy-start | bytes 835588
  34.4 4.4 %copy-start.14 = (bf16[272,512]{1,0:T(8,128)(2,1)}, bf16[272,512]{1,0:T(8,128)(2,1)S(1)}, u32[]{:S(2)}) copy-start(bf16[272,512]{1,0:T(8,128)(2,1)S(1)} %collective-permute-done.4.rest_4_) | copy-start | bytes 835588
  34.4 8.0 %collective-permute-start.6 = (bf16[272,512]{1,0:T(8,128)(2,1)S(1)}, bf16[272,512]{1,0:T(8,128)(2,1)S(1)}, u32[]{:S(2)}, u32[]{:S(2)}) collective-permute-start(bf16[272,512]{1,0:T(8,128)(2,1)S(1)} %get-tuple-element.39.rest_5_), channel_id=1, source_target_pairs={{0,4},{2,6},{4,8},{6,10},{8,12},{10,14},{1,5},{3,7},{5,9},{7,11},{... | collective-permute-start | bytes 835592 | tf_op jit(solution)/shard_map/ppermute | solution.py:131
  38.7 3.6 %copy-start.20 = (s32[256]{0:T(256)S(1)}, s32[256]{0:T(256)}, u32[]{:S(2)}) copy-start(s32[256]{0:T(256)} %param.15) | copy-start | bytes 3076
  38.7 3.6 %copy-start.21 = (f32[4]{0:T(128)S(1)}, f32[4]{0:T(128)}, u32[]{:S(2)}) copy-start(f32[4]{0:T(128)} %param.16) | copy-start | bytes 52
  38.7 7.7 %all-to-all-start = ((bf16[128,2,1024]{2,0,1:T(8,128)(2,1)}), bf16[128,2,1024]{2,0,1:T(8,128)(2,1)S(1)}, u32[]{:S(2)}, u32[]{:S(2)}) async-start(bf16[128,2,1024]{2,0,1:T(8,128)(2,1)} %bitcast.11), calls=%async_computation | async-start | bytes 1048576 | tf_op jit(solution)/shard_map/all_to_all | solution.py:144
  42.4 18.2 %copy-start.8 = (bf16[272,512]{1,0:T(8,128)(2,1)}, bf16[272,512]{1,0:T(8,128)(2,1)S(1)}, u32[]{:S(2)}) copy-start(bf16[272,512]{1,0:T(8,128)(2,1)S(1)} %collective-permute-done.6.rest_1_) | copy-start | bytes 835588
  42.4 20.2 %collective-permute-start.8 = (bf16[272,512]{1,0:T(8,128)(2,1)S(1)}, bf16[272,512]{1,0:T(8,128)(2,1)S(1)}, u32[]{:S(2)}, u32[]{:S(2)}) collective-permute-start(bf16[272,512]{1,0:T(8,128)(2,1)S(1)} %collective-permute-done.6.rest_1_), channel_id=1, source_target_pairs={{0,4},{2,6},{4,8},{6,10},{8,12},{10,14},{1,5},{3,7},{5,9},{7,11},{... | collective-permute-start | bytes 835592 | tf_op jit(solution)/shard_map/ppermute | solution.py:131
  57.3 8.9 %collective-permute-start.10 = (bf16[256,512]{1,0:T(8,128)(2,1)}, bf16[256,512]{1,0:T(8,128)(2,1)S(1)}, u32[]{:S(2)}, u32[]{:S(2)}) collective-permute-start(bf16[256,512]{1,0:T(8,128)(2,1)} %get-tuple-element.44), channel_id=1, source_target_pairs={{0,2},{4,6},{8,10},{12,14},{1,3},{5,7},{9,11},{13,15},{16,18},{20,... | collective-permute-start | bytes 786440 | tf_op jit(solution)/shard_map/ppermute | solution.py:131
  59.2 12.8 %collective-permute-start.5 = (bf16[272,512]{1,0:T(8,128)(2,1)S(1)}, bf16[272,512]{1,0:T(8,128)(2,1)S(1)}, u32[]{:S(2)}, u32[]{:S(2)}) collective-permute-start(bf16[272,512]{1,0:T(8,128)(2,1)S(1)} %get-tuple-element.39.rest_5_), channel_id=1, source_target_pairs={{0,2},{4,6},{8,10},{12,14},{1,3},{5,7},{9,11},{13,15},{16,18},{20,... | collective-permute-start | bytes 835592 | tf_op jit(solution)/shard_map/ppermute | solution.py:131
  60.5 36.8 %collective-permute-start.12 = (bf16[256,512]{1,0:T(8,128)(2,1)}, bf16[256,512]{1,0:T(8,128)(2,1)S(1)}, u32[]{:S(2)}, u32[]{:S(2)}) collective-permute-start(bf16[256,512]{1,0:T(8,128)(2,1)} %get-tuple-element.45), channel_id=1, source_target_pairs={{0,2},{4,6},{8,10},{12,14},{2,0},{6,4},{10,8},{14,12},{1,3},{5,7},... | collective-permute-start | bytes 786440 | tf_op jit(solution)/shard_map/ppermute | solution.py:131
  60.6 21.8 %collective-permute-start.7 = (bf16[272,512]{1,0:T(8,128)(2,1)S(1)}, bf16[272,512]{1,0:T(8,128)(2,1)S(1)}, u32[]{:S(2)}, u32[]{:S(2)}) collective-permute-start(bf16[272,512]{1,0:T(8,128)(2,1)S(1)} %collective-permute-done.6.rest_1_), channel_id=1, source_target_pairs={{0,2},{4,6},{8,10},{12,14},{2,0},{6,4},{10,8},{14,12},{1,3},{5,7},... | collective-permute-start | bytes 835592 | tf_op jit(solution)/shard_map/ppermute | solution.py:131
  62.6 4.7 %copy-start.9 = (bf16[272,512]{1,0:T(8,128)(2,1)}, bf16[272,512]{1,0:T(8,128)(2,1)S(1)}, u32[]{:S(2)}) copy-start(bf16[272,512]{1,0:T(8,128)(2,1)S(1)} %collective-permute-done.8.rest_3_) | copy-start | bytes 835588
  62.6 19.8 %collective-permute-start.9 = (bf16[272,512]{1,0:T(8,128)(2,1)S(1)}, bf16[272,512]{1,0:T(8,128)(2,1)S(1)}, u32[]{:S(2)}, u32[]{:S(2)}) collective-permute-start(bf16[272,512]{1,0:T(8,128)(2,1)S(1)} %collective-permute-done.8.rest_3_), channel_id=1, source_target_pairs={{2,0},{6,4},{10,8},{14,12},{3,1},{7,5},{11,9},{15,13},{18,16},{22,... | collective-permute-start | bytes 835592 | tf_op jit(solution)/shard_map/ppermute | solution.py:131
  66.1 5.9 %copy-start.22 = (bf16[256,512]{1,0:T(8,128)(2,1)S(1)}, bf16[256,512]{1,0:T(8,128)(2,1)}, u32[]{:S(2)}) copy-start(bf16[256,512]{1,0:T(8,128)(2,1)} %get-tuple-element.46) | copy-start | bytes 786436
  67.3 30.0 %collective-permute-start.11 = (bf16[256,512]{1,0:T(8,128)(2,1)S(1)}, bf16[256,512]{1,0:T(8,128)(2,1)S(1)}, u32[]{:S(2)}, u32[]{:S(2)}) collective-permute-start(bf16[256,512]{1,0:T(8,128)(2,1)S(1)} %add_convert_fusion.5), channel_id=1, source_target_pairs={{4,0},{6,2},{8,4},{10,6},{12,8},{14,10},{5,1},{7,3},{9,5},{11,7},{... | collective-permute-start | bytes 786440 | tf_op jit(solution)/shard_map/ppermute | solution.py:131
  72.0 10.4 %copy-start.15 = (bf16[272,512]{1,0:T(8,128)(2,1)}, bf16[272,512]{1,0:T(8,128)(2,1)S(1)}, u32[]{:S(2)}) copy-start(bf16[272,512]{1,0:T(8,128)(2,1)S(1)} %collective-permute-done.5.rest_0_) | copy-start | bytes 835588
  72.0 25.3 %copy-start.5 = (f32[256,512]{1,0:T(8,128)S(1)}, f32[256,512]{1,0:T(8,128)}, u32[]{:S(2)}) copy-start(f32[256,512]{1,0:T(8,128)} %get-tuple-element.42) | copy-start | bytes 1572868
  72.0 33.8 %collective-permute-start.14 = (bf16[256,512]{1,0:T(8,128)(2,1)S(1)}, bf16[256,512]{1,0:T(8,128)(2,1)S(1)}, u32[]{:S(2)}, u32[]{:S(2)}) collective-permute-start(bf16[256,512]{1,0:T(8,128)(2,1)S(1)} %copy-done.22), channel_id=1, source_target_pairs={{2,0},{6,4},{10,8},{14,12},{3,1},{7,5},{11,9},{15,13},{18,16},{22,... | collective-permute-start | bytes 786440 | tf_op jit(solution)/shard_map/ppermute | solution.py:131
  82.4 0.7 copy-start.16
  83.1 0.7 copy-start.17
  92.9 11.4 %collective-permute-start.15 = (bf16[256,512]{1,0:T(8,128)(2,1)}, bf16[256,512]{1,0:T(8,128)(2,1)S(1)}, u32[]{:S(2)}, u32[]{:S(2)}) collective-permute-start(bf16[256,512]{1,0:T(8,128)(2,1)} %get-tuple-element.50), channel_id=1, source_target_pairs={{0,2},{4,6},{8,10},{12,14},{1,3},{5,7},{9,11},{13,15},{16,18},{20,... | collective-permute-start | bytes 786440 | tf_op jit(solution)/shard_map/ppermute | solution.py:131
  97.3 1.6 %copy-start.24 = (bf16[256,512]{1,0:T(8,128)(2,1)S(1)}, bf16[256,512]{1,0:T(8,128)(2,1)}, u32[]{:S(2)}) copy-start(bf16[256,512]{1,0:T(8,128)(2,1)} %get-tuple-element.51) | copy-start | bytes 786436
  97.4 6.9 %copy-start.7 = (f32[256,512]{1,0:T(8,128)S(1)}, f32[256,512]{1,0:T(8,128)}, u32[]{:S(2)}) copy-start(f32[256,512]{1,0:T(8,128)} %get-tuple-element.49) | copy-start | bytes 1572868
  97.5 10.2 %collective-permute-start.13 = (bf16[256,512]{1,0:T(8,128)(2,1)S(1)}, bf16[256,512]{1,0:T(8,128)(2,1)S(1)}, u32[]{:S(2)}, u32[]{:S(2)}) collective-permute-start(bf16[256,512]{1,0:T(8,128)(2,1)S(1)} %add_convert_fusion.4), channel_id=1, source_target_pairs={{4,0},{6,2},{8,4},{10,6},{12,8},{14,10},{5,1},{7,3},{9,5},{11,7},{... | collective-permute-start | bytes 786440 | tf_op jit(solution)/shard_map/ppermute | solution.py:131
  98.9 11.0 %collective-permute-start.17 = (bf16[256,512]{1,0:T(8,128)(2,1)S(1)}, bf16[256,512]{1,0:T(8,128)(2,1)S(1)}, u32[]{:S(2)}, u32[]{:S(2)}) collective-permute-start(bf16[256,512]{1,0:T(8,128)(2,1)S(1)} %copy-done.24), channel_id=1, source_target_pairs={{0,2},{4,6},{8,10},{12,14},{2,0},{6,4},{10,8},{14,12},{1,3},{5,7},... | collective-permute-start | bytes 786440 | tf_op jit(solution)/shard_map/ppermute | solution.py:131
  104.3 3.4 %copy-start.3 = (f32[256,512]{1,0:T(8,128)S(1)}, f32[256,512]{1,0:T(8,128)}, u32[]{:S(2)}) copy-start(f32[256,512]{1,0:T(8,128)} %get-tuple-element.41) | copy-start | bytes 1572868
  104.4 8.4 %collective-permute-start.16 = (bf16[256,512]{1,0:T(8,128)(2,1)S(1)}, bf16[256,512]{1,0:T(8,128)(2,1)S(1)}, u32[]{:S(2)}, u32[]{:S(2)}) collective-permute-start(bf16[256,512]{1,0:T(8,128)(2,1)S(1)} %add_convert_fusion.2), channel_id=1, source_target_pairs={{4,0},{6,2},{8,4},{10,6},{12,8},{14,10},{5,1},{7,3},{9,5},{11,7},{... | collective-permute-start | bytes 786440 | tf_op jit(solution)/shard_map/ppermute | solution.py:131
  107.7 1.0 copy-start.23
  107.7 5.1 %copy-start.6 = (f32[256,512]{1,0:T(8,128)S(1)}, f32[256,512]{1,0:T(8,128)}, u32[]{:S(2)}) copy-start(f32[256,512]{1,0:T(8,128)} %get-tuple-element.48) | copy-start | bytes 1572868
  108.7 8.3 %collective-permute-start.19 = (bf16[256,512]{1,0:T(8,128)(2,1)S(1)}, bf16[256,512]{1,0:T(8,128)(2,1)S(1)}, u32[]{:S(2)}, u32[]{:S(2)}) collective-permute-start(bf16[256,512]{1,0:T(8,128)(2,1)S(1)} %copy-done.23), channel_id=1, source_target_pairs={{2,0},{6,4},{10,8},{14,12},{3,1},{7,5},{11,9},{15,13},{18,16},{22,... | collective-permute-start | bytes 786440 | tf_op jit(solution)/shard_map/ppermute | solution.py:131
  112.9 1.5 %copy-start.18 = (bf16[256,512]{1,0:T(8,128)(2,1)S(1)}, bf16[256,512]{1,0:T(8,128)(2,1)}, u32[]{:S(2)}) copy-start(bf16[256,512]{1,0:T(8,128)(2,1)} %get-tuple-element.38) | copy-start | bytes 786436
  112.9 1.5 %copy-start.19 = (bf16[256,512]{1,0:T(8,128)(2,1)S(1)}, bf16[256,512]{1,0:T(8,128)(2,1)}, u32[]{:S(2)}) copy-start(bf16[256,512]{1,0:T(8,128)(2,1)} %get-tuple-element.40) | copy-start | bytes 786436
  112.9 8.4 %collective-permute-start.18 = (bf16[256,512]{1,0:T(8,128)(2,1)S(1)}, bf16[256,512]{1,0:T(8,128)(2,1)S(1)}, u32[]{:S(2)}, u32[]{:S(2)}) collective-permute-start(bf16[256,512]{1,0:T(8,128)(2,1)S(1)} %add_convert_fusion.1), channel_id=1, source_target_pairs={{4,0},{6,2},{8,4},{10,6},{12,8},{14,10},{5,1},{7,3},{9,5},{11,7},{... | collective-permute-start | bytes 786440 | tf_op jit(solution)/shard_map/ppermute | solution.py:131
  114.4 6.9 %copy-start.4 = (f32[256,512]{1,0:T(8,128)S(1)}, f32[256,512]{1,0:T(8,128)}, u32[]{:S(2)}) copy-start(f32[256,512]{1,0:T(8,128)} %get-tuple-element.47) | copy-start | bytes 1572868
